TPU v7x, 512 devices: a whole 4x4x16 slice. The times are simulated.
512 devices in a mesh: dp: 16 (over x, y), seq: 32 (over z, core).
Axes of the slice: x: 4, y: 4, z: 16, core: 2. Of those that a mesh axis runs over, the one named last changes fastest.
Arguments:
- query_rows: bfloat16 [32, 2048, 2048], P('seq', 'dp'), may hold values from -8 to 8
- key_rows: bfloat16 [32, 2048, 2048], P('seq', 'dp'), may hold values from -8 to 8
- value_rows: bfloat16 [32, 2048, 2048], P('seq', 'dp'), may hold values from -6 to 6
- out_grad: bfloat16 [32, 2048, 3072], P('seq', 'dp'), may hold values from -96 to 96
- out_weight: bfloat16 [2, 2048, 3072], P(None, ('dp', 'seq')), may hold values from -0.125 to 0.125
- text_length: int32 [32], P('seq'), may hold values from 65 to 512
Outputs:
- query_grad: bfloat16 [32, 2048, 2048], P('seq', 'dp')
- key_grad: bfloat16 [32, 2048, 2048], P('seq', 'dp')
- value_grad: bfloat16 [32, 2048, 2048], P('seq', 'dp')
All inputs are finite; a program needn't handle non-finite values.
Results may differ from a plain program's by a relative error of at most 0.0076.
Values may be sent and summed in bfloat16 or wider, within the bound.
No kernel may reach another device: no remote copies, remote signals or barrier semaphores. Data moves between devices by JAX's collectives and lax.ppermute only.
A program may use at most 128 MiB of HBM per device.

v0:
```python
import math
import jax
import jax.numpy as jnp
from jax import lax
from jax.sharding import PartitionSpec as P

HEADS = 16
HEAD_DIM = 128
TXT = 512


def attention_grads(query_heads, key_heads, value_heads, grad_heads, key_valid):
    total_rows = query_heads.shape[0]
    block_rows = min(512, total_rows)
    factor = 1.0 / math.sqrt(query_heads.shape[2])
    key_total = jnp.zeros(key_heads.shape, jnp.float32)
    value_total = jnp.zeros(value_heads.shape, jnp.float32)
    query_parts = []
    for first_row in range(0, total_rows, block_rows):
        query_block = query_heads[first_row : first_row + block_rows]
        grad_block = grad_heads[first_row : first_row + block_rows]
        scores = (
            jnp.einsum("qhc,khc->hqk", query_block, key_heads, preferred_element_type=jnp.float32)
            * factor
        )
        scores = jnp.where(key_valid[None, None, :], scores, -jnp.inf)
        shifted = jnp.exp(scores - jnp.max(scores, axis=2, keepdims=True))
        attention = shifted / jnp.sum(shifted, axis=2, keepdims=True)
        value_total = value_total + jnp.einsum(
            "hqk,qhc->khc",
            attention.astype(jnp.bfloat16),
            grad_block,
            preferred_element_type=jnp.float32,
        )
        weight_grad = jnp.einsum(
            "qhc,khc->hqk", grad_block, value_heads, preferred_element_type=jnp.float32
        )
        row_dot = jnp.sum(attention * weight_grad, axis=2, keepdims=True)
        score_grad = (attention * (weight_grad - row_dot) * factor).astype(jnp.bfloat16)
        query_parts.append(
            jnp.einsum(
                "hqk,khc->qhc", score_grad, key_heads, preferred_element_type=jnp.float32
            ).astype(jnp.bfloat16)
        )
        key_total = key_total + jnp.einsum(
            "hqk,qhc->khc", score_grad, query_block, preferred_element_type=jnp.float32
        )
    return (
        jnp.concatenate(query_parts, axis=0),
        key_total.astype(jnp.bfloat16),
        value_total.astype(jnp.bfloat16),
    )


def per_device(query_rows, key_rows, value_rows, out_grad, out_weight, text_length):
    devices = lax.axis_size("dp")
    tok_rows = query_rows.shape[1]
    total_rows = tok_rows * devices
    positions = jnp.arange(total_rows)
    key_valid = (positions >= TXT) | (positions < text_length[0])

    def by_heads(array):
        return array[0].reshape(tok_rows, HEADS, HEAD_DIM)

    slot_text = (jnp.arange(devices) * tok_rows < TXT)[:, None, None]
    outgoing = jnp.where(slot_text, out_weight[0][None], out_weight[1][None])
    stream_rows = lax.all_to_all(outgoing, "dp", split_axis=0, concat_axis=0, tiled=True)
    projected = jnp.einsum(
        "te,kre->tkr",
        out_grad[0],
        lax.all_gather(stream_rows, "seq", axis=1, tiled=True),
        preferred_element_type=jnp.float32,
    )
    grad_tokens = projected.astype(jnp.bfloat16)
    query_heads, key_heads, value_heads, grad_heads = (
        lax.all_to_all(by_heads(query_rows), "dp", split_axis=1, concat_axis=0, tiled=True),
        lax.all_to_all(by_heads(key_rows), "dp", split_axis=1, concat_axis=0, tiled=True),
        lax.all_to_all(by_heads(value_rows), "dp", split_axis=1, concat_axis=0, tiled=True),
        lax.all_to_all(grad_tokens, "dp", split_axis=1, concat_axis=0, tiled=True),
    )
    query_grad, key_grad, value_grad = attention_grads(
        query_heads, key_heads, value_heads, grad_heads, key_valid
    )
    returned = (
        lax.all_to_all(query_grad, "dp", split_axis=0, concat_axis=1, tiled=True),
        lax.all_to_all(key_grad, "dp", split_axis=0, concat_axis=1, tiled=True),
        lax.all_to_all(value_grad, "dp", split_axis=0, concat_axis=1, tiled=True),
    )
    return (
        returned[0].reshape(1, tok_rows, HEADS * HEAD_DIM),
        returned[1].reshape(1, tok_rows, HEADS * HEAD_DIM),
        returned[2].reshape(1, tok_rows, HEADS * HEAD_DIM),
    )


def solution(mesh):
    in_specs = (
        P("seq", "dp", None),
        P("seq", "dp", None),
        P("seq", "dp", None),
        P("seq", "dp", None),
        P(None, ("dp", "seq"), None),
        P("seq"),
    )
    out_specs = (P("seq", "dp", None), P("seq", "dp", None), P("seq", "dp", None))
    return jax.shard_map(
        per_device, mesh=mesh, in_specs=in_specs, out_specs=out_specs, check_vma=False
    )
```

profile of v0, /device:TPU:32, one launch (start us, length us, event | category | flops | bytes accessed | tf_op | source)
XLA Modules:
  0.0 236.3 jit_solution(1114282494881835689)
XLA Ops:
  8.4 16.7 %all_to_all.110 = bf16[16,4,3072]{2,1,0:T(4,128)(2,1)S(1)} all-to-all(bf16[16,4,3072]{2,1,0:T(4,128)(2,1)S(1)} %broadcast_select_fusion), channel_id=1, replica_groups=mesh['dp'=16,'seq'=32] {'dp'}, dimensions={0} | all-to-all | bytes 786432 | tf_op jit(solution)/shard_map/all_to_all | solution.py:67
  26.0 2.0 copy.93
  28.0 3.7 %all-to-all-start = ((bf16[128,16,128]{0,2,1:T(8,128)(2,1)}), bf16[128,16,128]{0,2,1:T(8,128)(2,1)S(1)}, u32[]{:S(2)}, u32[]{:S(2)}) async-start(bf16[128,16,128]{0,2,1:T(8,128)(2,1)} %bitcast.1), calls=%async_computation | async-start | bytes 1048576 | tf_op jit(solution)/shard_map/all_to_all | solution.py:76
  32.7 9.3 %all-to-all-done = bf16[128,16,128]{0,2,1:T(8,128)(2,1)S(1)} async-done(((bf16[128,16,128]{0,2,1:T(8,128)(2,1)}), bf16[128,16,128]{0,2,1:T(8,128)(2,1)S(1)}, u32[]{:S(2)}, u32[]{:S(2)}) %all-to-all-start) | async-done | bytes 524320 | tf_op jit(solution)/shard_map/all_to_all | solution.py:76
  42.0 3.6 %all-to-all-start.1 = ((bf16[128,16,128]{0,2,1:T(8,128)(2,1)}), bf16[128,16,128]{0,2,1:T(8,128)(2,1)S(1)}, u32[]{:S(2)}, u32[]{:S(2)}) async-start(bf16[128,16,128]{0,2,1:T(8,128)(2,1)} %bitcast.5), calls=%async_computation.1 | async-start | bytes 1048576 | tf_op jit(solution)/shard_map/all_to_all | solution.py:77
  47.9 7.8 %all-to-all-done.1 = bf16[128,16,128]{0,2,1:T(8,128)(2,1)S(1)} async-done(((bf16[128,16,128]{0,2,1:T(8,128)(2,1)}), bf16[128,16,128]{0,2,1:T(8,128)(2,1)S(1)}, u32[]{:S(2)}, u32[]{:S(2)}) %all-to-all-start.1) | async-done | bytes 524320 | tf_op jit(solution)/shard_map/all_to_all | solution.py:77
  55.7 3.6 %all-to-all-start.4 = ((bf16[128,16,128]{0,2,1:T(8,128)(2,1)}), bf16[128,16,128]{0,2,1:T(8,128)(2,1)S(1)}, u32[]{:S(2)}, u32[]{:S(2)}) async-start(bf16[128,16,128]{0,2,1:T(8,128)(2,1)} %bitcast.17), calls=%async_computation.4 | async-start | bytes 1048576 | tf_op jit(solution)/shard_map/all_to_all | solution.py:78
  59.5 2.7 %fusion.36 = f32[512,2048]{1,0:T(8,128)} fusion(bf16[512,128]{1,0:T(8,128)(2,1)S(1)} %bitcast.148, bf16[2048,128]{1,0:T(8,128)(2,1)S(1)} %bitcast.120), kind=kOutput, calls=%fused_computation.66 | convolution fusion | flops 268435456 | bytes 4849664 | tf_op jit(solution)/shard_map/qhc,khc->hqk/dot_general | solution.py:23
  62.2 2.7 %fusion.35 = f32[512,2048]{1,0:T(8,128)} fusion(bf16[512,128]{1,0:T(8,128)(2,1)S(1)} %bitcast.142, bf16[2048,128]{1,0:T(8,128)(2,1)S(1)} %bitcast.121), kind=kOutput, calls=%fused_computation.65 | convolution fusion | flops 268435456 | bytes 4849664 | tf_op jit(solution)/shard_map/qhc,khc->hqk/dot_general | solution.py:23
  64.9 2.7 %fusion = (f32[512]{0:T(512)S(1)}, f32[512,2048]{1,0:T(8,128)}) fusion(pred[2048]{0:T(1024)(128)(4,1)S(1)} %fusion.27, bf16[512,128]{1,0:T(8,128)(2,1)S(1)} %bitcast.146, bf16[2048,128]{1,0:T(8,128)(2,1)S(1)} %bitcast.122), kind=kOutput, calls=%fused_computation.16 | convolution fusion | flops 271580672 | bytes 4853760 | tf_op jit(solution)/shard_map/qhc,khc->hqk/dot_general | solution.py:23
  67.6 45.6 %all-gather.2.cloned.1.call-done = bf16[16,128,3072]{2,0,1:T(8,128)(2,1)} async-done(((bf16[16,4,3072]{2,0,1:T(8,128)(2,1)}), bf16[16,128,3072]{2,0,1:T(8,128)(2,1)}) %all-gather.2.cloned.1.call-update) | async-done | bytes 12582928 | tf_op jit(solution)/shard_map/all_gather | solution.py:71
  113.2 6.5 %fusion.21 = bf16[128,16,128]{0,1,2:T(8,128)(2,1)S(1)} fusion(bf16[16,128,3072]{2,0,1:T(8,128)(2,1)} %all-gather.2.cloned.1.call-done, bf16[1,128,3072]{2,1,0:T(8,128)(2,1)S(1)} %copy-done), kind=kOutput, calls=%fused_computation.44 | convolution fusion | flops 1610874880 | bytes 13893632 | tf_op jit(solution)/shard_map/te,kre->tkr/dot_general | solution.py:68
  120.6 7.0 %all-to-all-start.3 = ((bf16[128,16,128]{0,2,1:T(8,128)(2,1)}), bf16[128,16,128]{0,2,1:T(8,128)(2,1)S(1)}, u32[]{:S(2)}, u32[]{:S(2)}) async-start(bf16[128,16,128]{0,2,1:T(8,128)(2,1)} %copy.98), calls=%async_computation.3 | async-start | bytes 1048576 | tf_op jit(solution)/shard_map/all_to_all | solution.py:79
  127.6 2.7 %fusion.34 = f32[512,2048]{1,0:T(8,128)} fusion(bf16[512,128]{1,0:T(8,128)(2,1)S(1)} %bitcast.144, bf16[2048,128]{1,0:T(8,128)(2,1)S(1)} %bitcast.123), kind=kOutput, calls=%fused_computation.64 | convolution fusion | flops 268435456 | bytes 4849664 | tf_op jit(solution)/shard_map/qhc,khc->hqk/dot_general | solution.py:23
  130.5 3.1 %fusion.5 = f32[512]{0:T(512)S(1)} fusion(f32[512,2048]{1,0:T(8,128)} %get-tuple-element.33, f32[512]{0:T(512)S(1)} %get-tuple-element.32, pred[2048]{0:T(1024)(128)(4,1)S(1)} %fusion.27), kind=kLoop, calls=%fused_computation.21 | loop fusion | flops 4193792 | bytes 4200448 | tf_op jit(solution)/shard_map/reduce_sum | solution.py:28
  133.7 5.8 %all-to-all-done.3 = bf16[128,16,128]{0,2,1:T(8,128)(2,1)S(1)} async-done(((bf16[128,16,128]{0,2,1:T(8,128)(2,1)}), bf16[128,16,128]{0,2,1:T(8,128)(2,1)S(1)}, u32[]{:S(2)}, u32[]{:S(2)}) %all-to-all-start.3) | async-done | bytes 524320 | tf_op jit(solution)/shard_map/all_to_all | solution.py:79
  140.6 3.0 %copy-done.2 = f32[512,2048]{1,0:T(8,128)S(1)} copy-done((f32[512,2048]{1,0:T(8,128)S(1)}, f32[512,2048]{1,0:T(8,128)}, u32[]{:S(2)}) %copy-start.2) | copy-done | bytes 4194328
  143.6 2.2 fusion.19
  145.8 1.6 copy-done.4
  148.6 3.9 %multiply_reduce_fusion.3 = (f32[512]{0:T(512)S(1)}, f32[512]{0:T(512)S(1)}, f32[512]{0:T(512)S(1)}, f32[512]{0:T(512)S(1)}, f32[512,2048]{1,0:T(8,128)}) fusion(f32[512]{0:T(512)S(1)} %fusion.5, f32[512]{0:T(512)S(1)} %get-tuple-element.32, f32[512,2048]{1,0:T(8,128)S(1)} %copy-done.2, pred[2048]{0:T(1024)(128)(4,1)S(1)} %fusion.27, ...), kind=kOutput, calls=%fused_computation.13 | convolution fusion | flops 284162048 | bytes 21641216 | tf_op jit(solution)/shard_map/qhc,khc->hqk/dot_general | solution.py:35
  153.4 4.5 %multiply_reduce_fusion.2 = (f32[512]{0:T(512)S(1)}, f32[512]{0:T(512)S(1)}, f32[512]{0:T(512)S(1)}, f32[512,2048]{1,0:T(8,128)}) fusion(f32[512]{0:T(512)S(1)} %fusion.7, f32[512]{0:T(512)S(1)} %get-tuple-element.10, f32[512,2048]{1,0:T(8,128)S(1)} %copy-done.3, pred[2048]{0:T(1024)(128)(4,1)S(1)} %fusion.27, f32[512]{0:T(512)S(1)} %get-tuple-element.11, ...), kind=kOutput, calls=%fused_computation.9 | convolution fusion | flops 283113984 | bytes 17448960 | tf_op jit(solution)/shard_map/qhc,khc->hqk/dot_general | solution.py:35
  157.9 7.4 %multiply_reduce_fusion.1 = (f32[512]{0:T(512)S(1)}, f32[512]{0:T(512)S(1)}, bf16[512,2048]{1,0:T(8,128)(2,1)}, f32[512,2048]{1,0:T(8,128)}) fusion(f32[512]{0:T(512)S(1)} %get-tuple-element.14, f32[512]{0:T(512)S(1)} %get-tuple-element.11, f32[512,2048]{1,0:T(8,128)S(1)} %copy-done.5, pred[2048]{0:T(1024)(128)(4,1)S(1)} %fusion.27, ...), kind=kOutput, calls=%fused_computation.5 | convolution fusion | flops 289405952 | bytes 27938816 | tf_op jit(solution)/shard_map/qhc,khc->hqk/dot_general | solution.py:35
  165.3 8.2 %multiply_convert_fusion.3 = (bf16[512,2048]{1,0:T(8,128)(2,1)S(1)}, bf16[512,2048]{1,0:T(8,128)(2,1)S(1)}, bf16[512,2048]{1,0:T(8,128)(2,1)S(1)}) fusion(f32[512,2048]{1,0:T(8,128)} %get-tuple-element.34, f32[512]{0:T(512)S(1)} %get-tuple-element.9, f32[512]{0:T(512)S(1)} %fusion.5, f32[512]{0:T(512)S(1)} %get-tuple-element.32, ...), kind=kLoop, calls=%fused_computation.12 | loop fusion | flops 25165824 | bytes 31477760 | tf_op jit(solution)/shard_map/convert_element_type | solution.py:39
  175.0 2.3 convolution_add_fusion.2
  186.0 3.6 %all-to-all-start.5 = ((bf16[16,2,8192]{2,1,0:T(2,128)(2,1)}), bf16[16,2,8192]{2,1,0:T(2,128)(2,1)S(1)}, u32[]{:S(2)}, u32[]{:S(2)}) async-start(bf16[16,2,8192]{2,1,0:T(2,128)(2,1)} %reshape.290), calls=%async_computation.5 | async-start | bytes 1048576 | tf_op jit(solution)/shard_map/all_to_all | solution.py:85
  189.6 4.8 %convolution_add_fusion.1 = f32[128,2048]{1,0:T(8,128)} fusion(f32[128,2048]{1,0:T(8,128)} %convolution_add_fusion.2, bf16[512,128]{1,0:T(8,128)(2,1)S(1)} %bitcast.153, f32[512,2048]{1,0:T(8,128)} %fusion.35, f32[512]{0:T(512)S(1)} %get-tuple-element.14, f32[512]{0:T(512)S(1)} %get-tuple-element.11, pred[2048]{0:T(1024)(128)(4,1)S(1)} %fusion.27), kind=kOutput, calls=%fused_computation.29 | convolution fusion | flops 273940480 | bytes 6428672 | tf_op jit(solution)/shard_map/hqk,qhc->khc/dot_general | solution.py:29
  194.4 5.8 %all-to-all-done.5 = bf16[16,2,8192]{2,1,0:T(2,128)(2,1)S(1)} async-done(((bf16[16,2,8192]{2,1,0:T(2,128)(2,1)}), bf16[16,2,8192]{2,1,0:T(2,128)(2,1)S(1)}, u32[]{:S(2)}, u32[]{:S(2)}) %all-to-all-start.5) | async-done | bytes 524320 | tf_op jit(solution)/shard_map/all_to_all | solution.py:85
  200.2 3.6 %all-to-all-start.6 = ((bf16[16,2,8192]{2,1,0:T(2,128)(2,1)}), bf16[16,2,8192]{2,1,0:T(2,128)(2,1)S(1)}, u32[]{:S(2)}, u32[]{:S(2)}) async-start(bf16[16,2,8192]{2,1,0:T(2,128)(2,1)} %reshape.292), calls=%async_computation.6 | async-start | bytes 1048576 | tf_op jit(solution)/shard_map/all_to_all | solution.py:86
  203.8 3.7 %fusion.14 = bf16[2048,1,128]{0,2,1:T(8,128)(2,1)S(1)} fusion(f32[128,2048]{1,0:T(8,128)} %convolution_add_fusion.1, bf16[512,128]{1,0:T(8,128)(2,1)S(1)} %bitcast.151, f32[512,2048]{1,0:T(8,128)} %fusion.36, f32[512]{0:T(512)S(1)} %get-tuple-element.15, f32[512]{0:T(512)S(1)} %get-tuple-element.12, pred[2048]{0:T(1024)(128)(4,1)S(1)} %fusion.27), kind=kOutput, calls=%fused_computation.36 | convolution fusion | flops 274202624 | bytes 5904384 | tf_op jit(solution)/shard_map/hqk,qhc->khc/dot_general | solution.py:29
  209.7 4.2 %all-to-all-done.6 = bf16[16,2,8192]{2,1,0:T(2,128)(2,1)S(1)} async-done(((bf16[16,2,8192]{2,1,0:T(2,128)(2,1)}), bf16[16,2,8192]{2,1,0:T(2,128)(2,1)S(1)}, u32[]{:S(2)}, u32[]{:S(2)}) %all-to-all-start.6) | async-done | bytes 524320 | tf_op jit(solution)/shard_map/all_to_all | solution.py:86
  213.9 3.6 %all-to-all-start.7 = ((bf16[16,2,8192]{2,1,0:T(2,128)(2,1)}), bf16[16,2,8192]{2,1,0:T(2,128)(2,1)S(1)}, u32[]{:S(2)}, u32[]{:S(2)}) async-start(bf16[16,2,8192]{2,1,0:T(2,128)(2,1)} %reshape.294), calls=%async_computation.7 | async-start | bytes 1048576 | tf_op jit(solution)/shard_map/all_to_all | solution.py:87
  221.3 6.2 %all-to-all-done.7 = bf16[16,2,8192]{2,1,0:T(2,128)(2,1)S(1)} async-done(((bf16[16,2,8192]{2,1,0:T(2,128)(2,1)}), bf16[16,2,8192]{2,1,0:T(2,128)(2,1)S(1)}, u32[]{:S(2)}, u32[]{:S(2)}) %all-to-all-start.7) | async-done | bytes 524320 | tf_op jit(solution)/shard_map/all_to_all | solution.py:87
  (91 shorter events, 27.3 us)
Async XLA Ops:
  7.2 106.0 %copy-start = (bf16[1,128,3072]{2,1,0:T(8,128)(2,1)S(1)}, bf16[1,128,3072]{2,1,0:T(8,128)(2,1)}, u32[]{:S(2)}) copy-start(bf16[1,128,3072]{2,1,0:T(8,128)(2,1)} %param.9) | copy-start | bytes 2359300
  7.2 24.6 %copy-start.12 = (bf16[1,128,2048]{2,1,0:T(8,128)(2,1)S(1)}, bf16[1,128,2048]{2,1,0:T(8,128)(2,1)}, u32[]{:S(2)}) copy-start(bf16[1,128,2048]{2,1,0:T(8,128)(2,1)} %param.7) | copy-start | bytes 1572868
  7.2 39.1 %copy-start.13 = (bf16[1,128,2048]{2,1,0:T(8,128)(2,1)S(1)}, bf16[1,128,2048]{2,1,0:T(8,128)(2,1)}, u32[]{:S(2)}) copy-start(bf16[1,128,2048]{2,1,0:T(8,128)(2,1)} %param.8) | copy-start | bytes 1572868
  7.2 106.0 %all-gather.2.cloned.1.call-start = ((), (), s32[]{:S(2)}) async-start(), calls=%async_computation.8 | async-start | bytes 12976128 | tf_op jit(solution)/shard_map/all_gather | solution.py:71
  28.0 14.0 %all-to-all-start = ((bf16[128,16,128]{0,2,1:T(8,128)(2,1)}), bf16[128,16,128]{0,2,1:T(8,128)(2,1)S(1)}, u32[]{:S(2)}, u32[]{:S(2)}) async-start(bf16[128,16,128]{0,2,1:T(8,128)(2,1)} %bitcast.1), calls=%async_computation | async-start | bytes 1048576 | tf_op jit(solution)/shard_map/all_to_all | solution.py:76
  42.0 13.6 %all-to-all-start.1 = ((bf16[128,16,128]{0,2,1:T(8,128)(2,1)}), bf16[128,16,128]{0,2,1:T(8,128)(2,1)S(1)}, u32[]{:S(2)}, u32[]{:S(2)}) async-start(bf16[128,16,128]{0,2,1:T(8,128)(2,1)} %bitcast.5), calls=%async_computation.1 | async-start | bytes 1048576 | tf_op jit(solution)/shard_map/all_to_all | solution.py:77
  47.5 17.4 %copy-start.10 = (bf16[4,128,1,128]{3,1,0,2:T(8,128)(2,1)}, bf16[4,128,1,128]{3,1,0,2:T(8,128)(2,1)S(1)}, u32[]{:S(2)}) copy-start(bf16[4,128,1,128]{3,1,0,2:T(8,128)(2,1)S(1)} %copy.104) | copy-start | bytes 393220
  47.9 17.0 %copy-start.8 = (bf16[4,128,1,128]{3,1,0,2:T(8,128)(2,1)}, bf16[4,128,1,128]{3,1,0,2:T(8,128)(2,1)S(1)}, u32[]{:S(2)}) copy-start(bf16[4,128,1,128]{3,1,0,2:T(8,128)(2,1)S(1)} %copy.94) | copy-start | bytes 393220
  55.7 64.9 %all-to-all-start.4 = ((bf16[128,16,128]{0,2,1:T(8,128)(2,1)}), bf16[128,16,128]{0,2,1:T(8,128)(2,1)S(1)}, u32[]{:S(2)}, u32[]{:S(2)}) async-start(bf16[128,16,128]{0,2,1:T(8,128)(2,1)} %bitcast.17), calls=%async_computation.4 | async-start | bytes 1048576 | tf_op jit(solution)/shard_map/all_to_all | solution.py:78
  120.6 18.9 %all-to-all-start.3 = ((bf16[128,16,128]{0,2,1:T(8,128)(2,1)}), bf16[128,16,128]{0,2,1:T(8,128)(2,1)S(1)}, u32[]{:S(2)}, u32[]{:S(2)}) async-start(bf16[128,16,128]{0,2,1:T(8,128)(2,1)} %copy.98), calls=%async_computation.3 | async-start | bytes 1048576 | tf_op jit(solution)/shard_map/all_to_all | solution.py:79
  139.8 3.8 %copy-start.2 = (f32[512,2048]{1,0:T(8,128)S(1)}, f32[512,2048]{1,0:T(8,128)}, u32[]{:S(2)}) copy-start(f32[512,2048]{1,0:T(8,128)} %get-tuple-element.33) | copy-start | bytes 12582916
  139.8 6.0 %copy-start.14 = (bf16[4,128,1,128]{3,1,0,2:T(8,128)(2,1)}, bf16[4,128,1,128]{3,1,0,2:T(8,128)(2,1)S(1)}, u32[]{:S(2)}) copy-start(bf16[4,128,1,128]{3,1,0,2:T(8,128)(2,1)S(1)} %get-tuple-element.23) | copy-start | bytes 393220
  139.8 13.6 %copy-start.18 = (bf16[4,128,1,128]{3,1,0,2:T(8,128)(2,1)}, bf16[4,128,1,128]{3,1,0,2:T(8,128)(2,1)S(1)}, u32[]{:S(2)}) copy-start(bf16[4,128,1,128]{3,1,0,2:T(8,128)(2,1)S(1)} %get-tuple-element.25) | copy-start | bytes 393220
  139.8 18.0 %copy-start.16 = (bf16[4,128,1,128]{3,1,0,2:T(8,128)(2,1)}, bf16[4,128,1,128]{3,1,0,2:T(8,128)(2,1)S(1)}, u32[]{:S(2)}) copy-start(bf16[4,128,1,128]{3,1,0,2:T(8,128)(2,1)S(1)} %get-tuple-element.24) | copy-start | bytes 393220
  140.6 17.3 %copy-start.6 = (f32[512,2048]{1,0:T(8,128)}, f32[512,2048]{1,0:T(8,128)S(1)}, u32[]{:S(2)}) copy-start(f32[512,2048]{1,0:T(8,128)S(1)} %fusion.37) | copy-start | bytes 12582916
  143.6 2.2 copy-start.3
  143.6 3.8 %copy-start.4 = (f32[512,2048]{1,0:T(8,128)S(1)}, f32[512,2048]{1,0:T(8,128)}, u32[]{:S(2)}) copy-start(f32[512,2048]{1,0:T(8,128)} %fusion.36) | copy-start | bytes 12582916
  143.6 5.0 %copy-start.5 = (f32[512,2048]{1,0:T(8,128)S(1)}, f32[512,2048]{1,0:T(8,128)}, u32[]{:S(2)}) copy-start(f32[512,2048]{1,0:T(8,128)} %fusion.35) | copy-start | bytes 12582916
  165.3 9.0 %copy-start.9 = (bf16[4,128,1,128]{3,1,0,2:T(8,128)(2,1)S(1)}, bf16[4,128,1,128]{3,1,0,2:T(8,128)(2,1)}, u32[]{:S(2)}) copy-start(bf16[4,128,1,128]{3,1,0,2:T(8,128)(2,1)} %copy-done.8) | copy-start | bytes 393220
  173.5 1.5 copy-start.19
  173.5 1.5 copy-start.20
  175.0 2.3 copy-start.7
  179.5 1.5 copy-start.11
  181.0 8.6 %copy-start.17 = (bf16[4,128,1,128]{3,1,0,2:T(8,128)(2,1)S(1)}, bf16[4,128,1,128]{3,1,0,2:T(8,128)(2,1)}, u32[]{:S(2)}) copy-start(bf16[4,128,1,128]{3,1,0,2:T(8,128)(2,1)} %copy-done.16) | copy-start | bytes 393220
  186.0 14.2 %all-to-all-start.5 = ((bf16[16,2,8192]{2,1,0:T(2,128)(2,1)}), bf16[16,2,8192]{2,1,0:T(2,128)(2,1)S(1)}, u32[]{:S(2)}, u32[]{:S(2)}) async-start(bf16[16,2,8192]{2,1,0:T(2,128)(2,1)} %reshape.290), calls=%async_computation.5 | async-start | bytes 1048576 | tf_op jit(solution)/shard_map/all_to_all | solution.py:85
  189.6 14.2 %copy-start.15 = (bf16[4,128,1,128]{3,1,0,2:T(8,128)(2,1)S(1)}, bf16[4,128,1,128]{3,1,0,2:T(8,128)(2,1)}, u32[]{:S(2)}) copy-start(bf16[4,128,1,128]{3,1,0,2:T(8,128)(2,1)} %copy-done.14) | copy-start | bytes 393220
  200.2 13.6 %all-to-all-start.6 = ((bf16[16,2,8192]{2,1,0:T(2,128)(2,1)}), bf16[16,2,8192]{2,1,0:T(2,128)(2,1)S(1)}, u32[]{:S(2)}, u32[]{:S(2)}) async-start(bf16[16,2,8192]{2,1,0:T(2,128)(2,1)} %reshape.292), calls=%async_computation.6 | async-start | bytes 1048576 | tf_op jit(solution)/shard_map/all_to_all | solution.py:86
  213.9 13.6 %all-to-all-start.7 = ((bf16[16,2,8192]{2,1,0:T(2,128)(2,1)}), bf16[16,2,8192]{2,1,0:T(2,128)(2,1)S(1)}, u32[]{:S(2)}, u32[]{:S(2)}) async-start(bf16[16,2,8192]{2,1,0:T(2,128)(2,1)} %reshape.294), calls=%async_computation.7 | async-start | bytes 1048576 | tf_op jit(solution)/shard_map/all_to_all | solution.py:87
  219.4 10.0 %copy-start.1 = (bf16[1,128,3072]{2,1,0:T(8,128)(2,1)S(1)}, bf16[1,128,3072]{2,1,0:T(8,128)(2,1)}, u32[]{:S(2)}) copy-start(bf16[1,128,3072]{2,1,0:T(8,128)(2,1)} %param.9) | copy-start | bytes 2359300
Sparse Core Ops, SparseCore 0:
  26.1 87.0 all-gather.1
where the time goes:
time: 237 us; the launch traced here: 236 us
  waiting for transfers between devices  84.8 us (36%)
  matrix products  52.5 us (22%)
  starting transfers between devices  28.6 us (12%)
  local copies, waits for them, and re-layouts  23.3 us (10%)
  blocking collectives  16.7 us (7%)
  other arithmetic  15.3 us (6%)
  between operations  15.2 us (6%)
    all_gather x1, waiting for transfers between devices, per_device(): lax.all_gather(stream_rows, 'seq', axis=1, tiled=True)  45.6 us
    unnamed x58, local copies, waits for them, and re-layouts  17.8 us
    all_to_all x1, blocking collectives, per_device(): lax.all_to_all(outgoing, 'dp', split_axis=0, concat_axis=0, tiled=True)  16.7 us
    dot_general x4, matrix products, attention_grads(): jnp.einsum('qhc,khc->hqk', grad_block, value_heads, preferred_element_typ...  16.4 us
    dot_general x4, matrix products, attention_grads(): jnp.einsum('hqk,qhc->khc', attention.astype(jnp.bfloat16), grad_block, pr...  13 us
    dot_general x4, matrix products, attention_grads(): jnp.einsum('qhc,khc->hqk', query_block, key_heads, preferred_element_type...  10.7 us
    all_to_all x1, waiting for transfers between devices, per_device(): lax.all_to_all(by_heads(query_rows), 'dp', split_axis=1, concat_axis=0, t...  9.29 us
    convert_element_type x1, other arithmetic, attention_grads(): (attention * (weight_grad - row_dot) * factor).astype(jnp.bfloat16)  8.21 us
  transfers between devices with their start and end apart: 8, of which 7 were waited for; matrix products, arithmetic and copies ran while one was open for 17% of the time, Pallas kernels for 0%

commit v1 on v0

--- a/solution.py
+++ b/solution.py
@@ -1,3 +1,4 @@
+import functools
 import math
 import jax
 import jax.numpy as jnp
@@ -7,6 +8,16 @@
 HEADS = 16
 HEAD_DIM = 128
 TXT = 512
+
+
+def streams_change(t0, axis_tag):
+    newest = jnp.concatenate(
+        lax.all_to_all(jnp.stack(lax.axis_size(axis_tag) * [t0]), axis_tag, 0, 0), axis=1
+    )
+    return newest
+
+
+expand_values = functools.partial(streams_change, axis_tag="seq")
 
 
 def attention_grads(query_heads, key_heads, value_heads, grad_heads, key_valid):
@@ -66,10 +77,7 @@
     outgoing = jnp.where(slot_text, out_weight[0][None], out_weight[1][None])
     stream_rows = lax.all_to_all(outgoing, "dp", split_axis=0, concat_axis=0, tiled=True)
     projected = jnp.einsum(
-        "te,kre->tkr",
-        out_grad[0],
-        lax.all_gather(stream_rows, "seq", axis=1, tiled=True),
-        preferred_element_type=jnp.float32,
+        "te,kre->tkr", out_grad[0], expand_values(stream_rows), preferred_element_type=jnp.float32
     )
     grad_tokens = projected.astype(jnp.bfloat16)
     query_heads, key_heads, value_heads, grad_heads = (

time: 237 us -> 780 us (3.29)
  waiting for transfers between devices: 84.8 us -> 570 us
  local copies, waits for them, and re-layouts: 23.3 us -> 64.6 us
  starting transfers between devices: 28.6 us -> 51.4 us
  between operations: 15.2 us -> 1.81 us
    all_to_all x1 -> x2, waiting for transfers between devices: 9.29 us -> 547 us  [the longest x1 539 us: streams_change(): lax.all_to_all(jnp.stack(lax.axis_size(axis_tag) * [t0]), axis_tag, 0, 0)]
    all_gather x1 -> x0, waiting for transfers between devices: 45.6 us -> none  [per_device(): lax.all_gather(stream_rows, 'seq', axis=1, tiled=True)]
    reshape x0 -> x2, local copies, waits for them, and re-layouts: none -> 31.4 us  [streams_change(): jnp.concatenate(lax.all_to_all(jnp.stack(lax.axis_size(axis_tag) * [t0]),...]
    all_to_all x1 -> x2, starting transfers between devices: 3.71 us -> 22.6 us  [the longest x1 15.5 us: streams_change(): lax.all_to_all(jnp.stack(lax.axis_size(axis_tag) * [t0]), axis_tag, 0, 0)]
    unnamed x58 -> x66, local copies, waits for them, and re-layouts: 17.8 us -> 22.4 us
  transfers between devices with their start and end apart: 8 -> 8, of which waited for: 7 -> 6; matrix products, arithmetic and copies ran while one was open for 17% -> 13% of each run, Pallas kernels for 0% -> 0%
where the time goes in v1:
time: 780 us; the launch traced here: 778 us
  waiting for transfers between devices  570 us (73%)
  local copies, waits for them, and re-layouts  64.6 us (8%)
  matrix products  59.4 us (8%)
  starting transfers between devices  51.4 us (7%)
  other arithmetic  17 us (2%)
  blocking collectives  13.3 us (2%)
    all_to_all x1, waiting for transfers between devices, streams_change(): lax.all_to_all(jnp.stack(lax.axis_size(axis_tag) * [t0]), axis_tag, 0, 0)  539 us
    reshape x2, local copies, waits for them, and re-layouts, streams_change(): jnp.concatenate(lax.all_to_all(jnp.stack(lax.axis_size(axis_tag) * [t0]),...  31.4 us
    unnamed x66, local copies, waits for them, and re-layouts  22.4 us
    dot_general x4, matrix products, attention_grads(): jnp.einsum('qhc,khc->hqk', grad_block, value_heads, preferred_element_typ...  21.6 us
  transfers between devices with their start and end apart: 8, of which 6 were waited for; matrix products, arithmetic and copies ran while one was open for 13% of the time, Pallas kernels for 0%

profile of v1, /device:TPU:32, one launch (start us, length us, event | category | flops | bytes accessed | tf_op | source)
XLA Modules:
  0.0 777.9 jit_solution(3538668867452895307)
XLA Ops:
  2.5 7.0 all-to-all-start.2
  11.5 7.8 all-to-all-done.2
  19.3 3.7 all-to-all-start.1
  24.4 9.0 %all-to-all-done.1 = bf16[128,16,128]{0,2,1:T(8,128)(2,1)S(1)} async-done(((bf16[128,16,128]{0,2,1:T(8,128)(2,1)}), bf16[128,16,128]{0,2,1:T(8,128)(2,1)S(1)}, u32[]{:S(2)}, u32[]{:S(2)}) %all-to-all-start.1) | async-done | bytes 524320 | tf_op jit(solution)/shard_map/all_to_all | solution.py:85
  33.3 13.3 %all_to_all.115 = bf16[128,16,128]{0,2,1:T(8,128)(2,1)S(1)} all-to-all(bf16[128,16,128]{0,2,1:T(8,128)(2,1)S(1)} %bitcast.140), channel_id=1, replica_groups=mesh['dp'=16,'seq'=32] {'dp'}, dimensions={1} | all-to-all | bytes 1048576 | tf_op jit(solution)/shard_map/all_to_all | solution.py:84
  46.7 6.8 stack.2
  53.5 15.5 %all-to-all-start.3 = ((bf16[32,16,4,3072]{3,2,1,0:T(4,128)(2,1)}), bf16[32,16,4,3072]{3,2,1,0:T(4,128)(2,1)}, u32[]{:S(2)}, u32[]{:S(2)}) async-start(bf16[32,16,4,3072]{3,2,1,0:T(4,128)(2,1)} %stack.2), calls=%async_computation.3 | async-start | bytes 25165824 | tf_op jit(solution)/shard_map/all_to_all | solution.py:15
  71.6 2.8 fusion.34
  74.4 2.7 fusion.35
  77.0 2.7 fusion
  79.7 539.1 %all-to-all-done.3 = bf16[32,16,4,3072]{3,2,1,0:T(4,128)(2,1)} async-done(((bf16[32,16,4,3072]{3,2,1,0:T(4,128)(2,1)}), bf16[32,16,4,3072]{3,2,1,0:T(4,128)(2,1)}, u32[]{:S(2)}, u32[]{:S(2)}) %all-to-all-start.3) | async-done | bytes 12582944 | tf_op jit(solution)/shard_map/all_to_all | solution.py:15
  618.8 3.6 all-to-all-start.5
  622.3 11.3 %copy.76 = bf16[16,32,4,3072]{3,2,1,0:T(4,128)(2,1)} copy(bf16[16,32,4,3072]{3,2,0,1:T(4,128)(2,1)} %bitcast.11) | data formatting | bytes 25165824 | tf_op jit(solution)/shard_map/reshape | solution.py:14
  633.6 20.2 %reshape.287 = bf16[16,128,3072]{2,1,0:T(8,128)(2,1)} reshape(bf16[16,32,4,3072]{3,2,1,0:T(4,128)(2,1)} %copy.76) | data formatting | bytes 25165824 | tf_op jit(solution)/shard_map/reshape | solution.py:14
  653.8 7.2 fusion.21
  661.0 7.2 all-to-all-start.4
  668.2 2.6 fusion.36
  671.1 3.1 fusion.5
  674.3 4.9 all-to-all-done.4
  679.4 4.6 fusion.19
  686.9 3.9 multiply_reduce_fusion.3
  692.1 2.8 fusion.37
  695.6 2.7 convolution_add_fusion.2
  699.4 4.4 multiply_reduce_fusion.2
  709.1 3.8 all-to-all-start.8
  712.9 10.6 %multiply_reduce_fusion.1 = (f32[512]{0:T(512)S(1)}, f32[512]{0:T(512)S(1)}, bf16[512,2048]{1,0:T(8,128)(2,1)S(1)}, f32[512,2048]{1,0:T(8,128)}) fusion(f32[512]{0:T(512)S(1)} %get-tuple-element.11, f32[512]{0:T(512)S(1)} %get-tuple-element.8, f32[512,2048]{1,0:T(8,128)} %fusion.35, pred[2048]{0:T(1024)(128)(4,1)S(1)} %fusion.27, f32[512,2048]{1,0:T(8,128)} %fusion.37, ...), kind=kOutput, calls=%fused_computation.5 | convolution fusion | flops 289405952 | bytes 27938816 | tf_op jit(solution)/shard_map/qhc,khc->hqk/dot_general | solution.py:46
  725.9 7.3 multiply_convert_fusion.3
  737.4 2.7 reduce.25
  745.2 7.0 all-to-all-start.7
  757.2 5.2 all-to-all-done.7
  762.4 3.6 all-to-all-start.6
  771.6 4.5 all-to-all-done.6
  (102 shorter events, 42.8 us)
Async XLA Ops:
  0.6 653.2 %copy-start = (bf16[1,128,3072]{2,1,0:T(8,128)(2,1)S(1)}, bf16[1,128,3072]{2,1,0:T(8,128)(2,1)}, u32[]{:S(2)}) copy-start(bf16[1,128,3072]{2,1,0:T(8,128)(2,1)} %param.9) | copy-start | bytes 2359300
  2.5 16.9 %all-to-all-start.2 = ((bf16[16,4,3072]{2,1,0:T(4,128)(2,1)}), bf16[16,4,3072]{2,1,0:T(4,128)(2,1)S(1)}, u32[]{:S(2)}, u32[]{:S(2)}) async-start(bf16[16,4,3072]{2,1,0:T(4,128)(2,1)} %broadcast_select_fusion), calls=%async_computation.2 | async-start | bytes 786432 | tf_op jit(solution)/shard_map/all_to_all | solution.py:78
  19.3 14.0 %all-to-all-start.1 = ((bf16[128,16,128]{0,2,1:T(8,128)(2,1)}), bf16[128,16,128]{0,2,1:T(8,128)(2,1)S(1)}, u32[]{:S(2)}, u32[]{:S(2)}) async-start(bf16[128,16,128]{0,2,1:T(8,128)(2,1)} %bitcast.5), calls=%async_computation.1 | async-start | bytes 1048576 | tf_op jit(solution)/shard_map/all_to_all | solution.py:85
  53.5 16.2 %copy-start.22 = (bf16[1,128,2048]{2,1,0:T(8,128)(2,1)S(1)}, bf16[1,128,2048]{2,1,0:T(8,128)(2,1)}, u32[]{:S(2)}) copy-start(bf16[1,128,2048]{2,1,0:T(8,128)(2,1)} %param.8) | copy-start | bytes 1572868
  53.5 565.3 %all-to-all-start.3 = ((bf16[32,16,4,3072]{3,2,1,0:T(4,128)(2,1)}), bf16[32,16,4,3072]{3,2,1,0:T(4,128)(2,1)}, u32[]{:S(2)}, u32[]{:S(2)}) async-start(bf16[32,16,4,3072]{3,2,1,0:T(4,128)(2,1)} %stack.2), calls=%async_computation.3 | async-start | bytes 25165824 | tf_op jit(solution)/shard_map/all_to_all | solution.py:15
  71.2 5.9 copy-start.18
  71.3 5.7 copy-start.16
  71.6 596.6 %copy-start.20 = (bf16[4,128,1,128]{3,1,0,2:T(8,128)(2,1)}, bf16[4,128,1,128]{3,1,0,2:T(8,128)(2,1)S(1)}, u32[]{:S(2)}) copy-start(bf16[4,128,1,128]{3,1,0,2:T(8,128)(2,1)S(1)} %copy.84) | copy-start | bytes 393220
  618.8 42.3 %all-to-all-start.5 = ((bf16[128,16,128]{0,2,1:T(8,128)(2,1)}), bf16[128,16,128]{0,2,1:T(8,128)(2,1)S(1)}, u32[]{:S(2)}, u32[]{:S(2)}) async-start(bf16[128,16,128]{0,2,1:T(8,128)(2,1)} %bitcast.18), calls=%async_computation.5 | async-start | bytes 1048576 | tf_op jit(solution)/shard_map/all_to_all | solution.py:86
  661.0 18.2 %all-to-all-start.4 = ((bf16[128,16,128]{0,2,1:T(8,128)(2,1)}), bf16[128,16,128]{0,2,1:T(8,128)(2,1)S(1)}, u32[]{:S(2)}, u32[]{:S(2)}) async-start(bf16[128,16,128]{0,2,1:T(8,128)(2,1)} %fusion.21), calls=%async_computation.4 | async-start | bytes 1048576 | tf_op jit(solution)/shard_map/all_to_all | solution.py:87
  679.4 4.7 copy-start.2
  679.4 4.9 copy-start.6
  679.4 6.3 copy-start.8
  679.4 7.5 copy-start.11
  690.8 22.1 %copy-start.23 = (f32[512]{0:T(512)}, f32[512]{0:T(512)S(1)}, u32[]{:S(2)}) copy-start(f32[512]{0:T(512)S(1)} %get-tuple-element.8) | copy-start | bytes 6148
  690.8 22.1 %copy-start.24 = (f32[512]{0:T(512)}, f32[512]{0:T(512)S(1)}, u32[]{:S(2)}) copy-start(f32[512]{0:T(512)S(1)} %get-tuple-element.9) | copy-start | bytes 6148
  692.1 3.5 copy-start.7
  695.6 2.7 copy-start.9
  695.6 3.8 copy-start.12
  709.1 36.1 %all-to-all-start.8 = ((bf16[16,2,8192]{2,1,0:T(2,128)(2,1)}), bf16[16,2,8192]{2,1,0:T(2,128)(2,1)S(1)}, u32[]{:S(2)}, u32[]{:S(2)}) async-start(bf16[16,2,8192]{2,1,0:T(2,128)(2,1)} %reshape.304), calls=%async_computation.8 | async-start | bytes 1048576 | tf_op jit(solution)/shard_map/all_to_all | solution.py:95
  712.9 10.6 %copy-start.3 = (f32[512,2048]{1,0:T(8,128)S(1)}, f32[512,2048]{1,0:T(8,128)}, u32[]{:S(2)}) copy-start(f32[512,2048]{1,0:T(8,128)} %get-tuple-element.30) | copy-start | bytes 12582916
  712.9 10.6 %copy-start.10 = (f32[512,2048]{1,0:T(8,128)S(1)}, f32[512,2048]{1,0:T(8,128)}, u32[]{:S(2)}) copy-start(f32[512,2048]{1,0:T(8,128)} %fusion.35) | copy-start | bytes 12582916
  712.9 13.0 %copy-start.13 = (f32[512,2048]{1,0:T(8,128)S(1)}, f32[512,2048]{1,0:T(8,128)}, u32[]{:S(2)}) copy-start(f32[512,2048]{1,0:T(8,128)} %fusion.36) | copy-start | bytes 12582916
  723.5 10.5 %copy-start.14 = (bf16[512,2048]{1,0:T(8,128)(2,1)}, bf16[512,2048]{1,0:T(8,128)(2,1)S(1)}, u32[]{:S(2)}) copy-start(bf16[512,2048]{1,0:T(8,128)(2,1)S(1)} %get-tuple-element.28) | copy-start | bytes 6291460
  725.9 7.4 copy-start.19
  733.3 1.8 copy-start.5
  733.3 2.6 copy-start.4
  734.3 1.5 copy-start.21
  742.8 11.8 %copy-start.15 = (bf16[512,2048]{1,0:T(8,128)(2,1)S(1)}, bf16[512,2048]{1,0:T(8,128)(2,1)}, u32[]{:S(2)}) copy-start(bf16[512,2048]{1,0:T(8,128)(2,1)} %copy-done.14) | copy-start | bytes 6291460
  745.2 17.2 %all-to-all-start.7 = ((bf16[16,2,8192]{2,1,0:T(2,128)(2,1)}), bf16[16,2,8192]{2,1,0:T(2,128)(2,1)}, u32[]{:S(2)}, u32[]{:S(2)}) async-start(bf16[16,2,8192]{2,1,0:T(2,128)(2,1)} %reshape.302), calls=%async_computation.7 | async-start | bytes 1048576 | tf_op jit(solution)/shard_map/all_to_all | solution.py:94
  762.4 13.6 %all-to-all-start.6 = ((bf16[16,2,8192]{2,1,0:T(2,128)(2,1)}), bf16[16,2,8192]{2,1,0:T(2,128)(2,1)S(1)}, u32[]{:S(2)}, u32[]{:S(2)}) async-start(bf16[16,2,8192]{2,1,0:T(2,128)(2,1)} %reshape.300), calls=%async_computation.6 | async-start | bytes 1048576 | tf_op jit(solution)/shard_map/all_to_all | solution.py:93
  767.9 10.0 %copy-start.1 = (bf16[1,128,3072]{2,1,0:T(8,128)(2,1)S(1)}, bf16[1,128,3072]{2,1,0:T(8,128)(2,1)}, u32[]{:S(2)}) copy-start(bf16[1,128,3072]{2,1,0:T(8,128)(2,1)} %param.9) | copy-start | bytes 2359300
  (1 other events, 1.1 us)
